TPU v7x, 512 devices: a whole 4x8x8 slice. The times are simulated.
512 devices in a mesh: dp: 64 (over x, y, core), mp: 8 (over z).
Axes of the slice: x: 4, y: 8, z: 8, core: 2. Of those that a mesh axis runs over, the one named last changes fastest.
Arguments:
- corpus: bfloat16 [8192, 16, 320], P('dp'), may hold values from -6 to 6
- picks: int32 [64, 64], P('dp'), may hold values from 0 to 127
- lengths: int32 [8192], P('dp'), may hold values from 1 to 16, 98304 in all
- langs: int32 [8192], P('dp'), may hold values from 0 to 127
- w_in: bfloat16 [320, 1536], P(None, 'mp'), may hold values from -0.3125 to 0.3125
- lang_table: bfloat16 [128, 1536], P(None, 'mp'), may hold values from -3 to 3
- ln_gain: float32 [1536], P('mp'), may hold values from 0.1 to 1.9
- w_pw1: bfloat16 [1536, 2, 1536], P('dp', None, 'mp'), may hold values from -0.15625 to 0.15625
- kernel: float32 [31, 1536], P(None, 'mp'), may hold values from -1.5 to 1.5
- bn_gain: float32 [1536], P('mp'), may hold values from 0.1 to 1.9
- bn_bias: float32 [1536], P('mp'), may hold values from -3 to 3
- w_pw2: bfloat16 [1536, 1536], P('dp', 'mp'), may hold values from -0.15625 to 0.15625
- cotangent: bfloat16 [65536, 1536], P('dp', 'mp'), may hold values from -6 to 6
Outputs:
- encoded: bfloat16 [65536, 1536], P('dp', 'mp')
- grad_pw1: float32 [1536, 2, 1536], P('dp', None, 'mp')
- grad_pw2: float32 [1536, 1536], P('dp', 'mp')
- grad_kernel: float32 [31, 1536], P(None, 'mp')
- grad_bn_gain: float32 [1536], P('mp')
- grad_bn_bias: float32 [1536], P('mp')
Inputs may be any that keep to these rules, and one draw needn't show every extreme that they name: `picks`: each trainer takes one block of every shard; a shard may give the same block to several trainers.
All inputs are finite; a program needn't handle non-finite values. No bound on the sum of `lengths` on one device may be relied on, other than what follows from the above.
Results may differ from a plain program's by a relative error of at most 0.0057.
Values may be sent and summed in bfloat16 or wider, within the bound.
No kernel may reach another device: no remote copies, remote signals or barrier semaphores. Data moves between devices by JAX's collectives and lax.ppermute only.
A program may use at most 64 MiB of HBM per device.

v0:
```python
import jax
import jax.numpy as jnp
from jax import lax
from jax.sharding import Mesh, PartitionSpec as P

EPS = 1e-05


def depth_conv(values, taps, frames):
    chans = values.shape[1]
    shaped = values.reshape(-1, frames, chans)
    margin = taps.shape[0] // 2
    padded = jnp.pad(shaped, ((0, 0), (margin, margin), (0, 0)))
    total = jnp.zeros(shaped.shape, jnp.float32)
    for step in range(taps.shape[0]):
        total = total + taps[step] * padded[:, step : step + frames]
    return total.reshape(values.shape)


def depth_back(grads, taps, frames):
    chans = grads.shape[1]
    shaped = grads.reshape(-1, frames, chans)
    margin = taps.shape[0] // 2
    padded = jnp.pad(shaped, ((0, 0), (margin, margin), (0, 0)))
    total = jnp.zeros(shaped.shape, jnp.float32)
    for step in range(taps.shape[0]):
        begin = 2 * margin - step
        total = total + taps[step] * padded[:, begin : begin + frames]
    return total.reshape(grads.shape)


def kernel_terms(grads, values, width, frames):
    chans = values.shape[1]
    shaped = values.reshape(-1, frames, chans)
    grad_shaped = grads.reshape(-1, frames, chans)
    margin = width // 2
    padded = jnp.pad(shaped, ((0, 0), (margin, margin), (0, 0)))
    rows_out = []
    for step in range(width):
        rows_out.append(jnp.sum(grad_shaped * padded[:, step : step + frames], axis=(0, 1)))
    return jnp.stack(rows_out, 0)


DP_AXES = ("x", "y", "c")


def dp_sum(value):
    for name in reversed(DP_AXES):
        value = lax.psum(value, name)
    return value


def contract_rows(left, right):
    return lax.dot_general(
        left, right, (((0,), (0,)), ((), ())), preferred_element_type=jnp.float32
    )


def on_device(
    corpus,
    picks,
    lengths,
    langs,
    w_in,
    lang_table,
    ln_gain,
    w_pw1,
    kernel,
    bn_gain,
    bn_bias,
    w_pw2,
    cotangent,
):
    model_width = w_pw2.shape[0] * lax.axis_size(DP_AXES)
    chosen = picks[0]
    blocks = jnp.take(corpus, chosen, axis=0)
    lens_send = jnp.take(lengths, chosen)
    lang_send = jnp.take(langs, chosen)
    received, lens, lang = (
        lax.all_to_all(blocks, DP_AXES, split_axis=0, concat_axis=0, tiled=True),
        lax.all_to_all(lens_send, DP_AXES, split_axis=0, concat_axis=0, tiled=True),
        lax.all_to_all(lang_send, DP_AXES, split_axis=0, concat_axis=0, tiled=True),
    )
    frames = received.shape[1]
    valid = (
        (jnp.arange(frames, dtype=jnp.int32)[None, :] < lens[:, None])
        .astype(jnp.float32)
        .reshape(-1)
    )
    valid_col = valid[:, None]
    mel = received.reshape(-1, received.shape[2]) * valid_col.astype(jnp.bfloat16)
    onehot = (lang[:, None] == jnp.arange(lang_table.shape[0], dtype=jnp.int32)[None, :]).astype(
        jnp.bfloat16
    )
    lang_rows = jnp.dot(onehot, lang_table, preferred_element_type=jnp.float32)
    inputs = jnp.dot(mel, w_in, preferred_element_type=jnp.float32) + jnp.repeat(
        lang_rows, frames, axis=0
    )
    row_sum, row_sq = lax.psum((jnp.sum(inputs, 1), jnp.sum(inputs * inputs, 1)), "mp")
    mean = row_sum / model_width
    var = row_sq / model_width - mean * mean
    normed_in = ((inputs - mean[:, None]) * lax.rsqrt(var + EPS)[:, None] * ln_gain).astype(
        jnp.bfloat16
    )
    weights_one = lax.all_gather(w_pw1, DP_AXES, axis=0, tiled=True).reshape(model_width, -1)
    half = weights_one.shape[1] // 2
    normed_full = lax.all_gather(normed_in, "mp", axis=1, tiled=True)
    pre = jnp.dot(normed_full, weights_one, preferred_element_type=jnp.float32)
    linear_part = pre[:, :half]
    gate_part = pre[:, half:]
    gate_sig = jax.nn.sigmoid(gate_part)
    glu_out = linear_part * gate_sig * valid_col
    conv_out = depth_conv(glu_out, kernel, frames)
    sum_conv, sum_sq, count = dp_sum(
        (
            jnp.sum(valid_col * conv_out, 0),
            jnp.sum(valid_col * conv_out * conv_out, 0),
            jnp.sum(valid),
        )
    )
    mu_conv = sum_conv / count
    var_conv = sum_sq / count - mu_conv * mu_conv
    inv_std = lax.rsqrt(var_conv + EPS)
    normed_conv = (conv_out - mu_conv) * inv_std
    act = normed_conv * bn_gain + bn_bias
    act_sig = jax.nn.sigmoid(act)
    hidden = (valid_col * act * act_sig).astype(jnp.bfloat16)
    weights_two = lax.all_gather(w_pw2, DP_AXES, axis=0, tiled=True)
    hidden_full = lax.all_gather(hidden, "mp", axis=1, tiled=True)
    encoded = (
        inputs + jnp.dot(hidden_full, weights_two, preferred_element_type=jnp.float32)
    ).astype(jnp.bfloat16)
    grad_pw2 = lax.psum_scatter(
        contract_rows(hidden_full, cotangent), DP_AXES, scatter_dimension=0, tiled=True
    )
    cot_full = lax.all_gather(cotangent, "mp", axis=1, tiled=True)
    weights_rows = lax.all_to_all(weights_two, "mp", split_axis=0, concat_axis=1, tiled=True)
    dhidden = lax.dot_general(
        cot_full, weights_rows, (((1,), (1,)), ((), ())), preferred_element_type=jnp.float32
    )
    dact = dhidden * valid_col * act_sig * (1.0 + act * (1.0 - act_sig))
    grad_bias, grad_gain = dp_sum((jnp.sum(dact, 0), jnp.sum(dact * normed_conv, 0)))
    dconv = (
        valid_col * inv_std * bn_gain * (dact - grad_bias / count - normed_conv * grad_gain / count)
    )
    grad_kernel = dp_sum(kernel_terms(dconv, glu_out, kernel.shape[0], frames))
    dglu = depth_back(dconv, kernel, frames)
    dlin = dglu * valid_col * gate_sig
    dgate = dglu * valid_col * linear_part * gate_sig * (1.0 - gate_sig)
    dpre = jnp.concatenate([dlin, dgate], 1).astype(jnp.bfloat16)
    grad_pw1 = lax.psum_scatter(
        contract_rows(normed_full, dpre), DP_AXES, scatter_dimension=0, tiled=True
    )
    grad_pw1 = grad_pw1.reshape(grad_pw1.shape[0], 2, half)
    return (encoded, grad_pw1, grad_pw2, grad_kernel, grad_gain, grad_bias)


def dp_shape(mesh):
    along = mesh.devices[:, 0]
    try:
        xs = len({d.coords[0] for d in along})
        ys = len({d.coords[1] for d in along})
    except AttributeError:
        xs, ys = (1, 1)
    cores = mesh.shape["dp"] // (xs * ys)
    return (xs, ys, cores)


def solution(mesh):
    xs, ys, cores = dp_shape(mesh)
    fine = Mesh(mesh.devices.reshape(xs, ys, cores, mesh.shape["mp"]), DP_AXES + ("mp",))
    D = DP_AXES
    return jax.shard_map(
        on_device,
        mesh=fine,
        in_specs=(
            P(D, None, None),
            P(D, None),
            P(D),
            P(D),
            P(None, "mp"),
            P(None, "mp"),
            P("mp"),
            P(D, None, "mp"),
            P(None, "mp"),
            P("mp"),
            P("mp"),
            P(D, "mp"),
            P(D, "mp"),
        ),
        out_specs=(P(D, "mp"), P(D, None, "mp"), P(D, "mp"), P(None, "mp"), P("mp"), P("mp")),
        check_vma=False,
    )
```

profile of v0, /device:TPU:16, one launch (start us, length us, event | category | flops | bytes accessed | tf_op | source)
XLA Modules:
  0.0 642.6 jit_solution(16453349370406005419)
XLA Ops:
  10.7 10.5 %all-to-all-start.1 = ((s32[64,1,1]{2,1,0:T(1,128)}), s32[64,1,1]{2,1,0:T(1,128)S(1)}, u32[]{:S(2)}, u32[]{:S(2)}) async-start(s32[64,1,1]{2,1,0:T(1,128)} %copy.39), calls=%async_computation.1 | async-start | bytes 65536 | tf_op jit(solution)/shard_map/all_to_all | solution.py:81
  28.8 8.4 %all-to-all-start.2 = ((s32[64,1,1]{2,1,0:T(1,128)}), s32[64,1,1]{2,1,0:T(1,128)S(1)}, u32[]{:S(2)}, u32[]{:S(2)}) async-start(s32[64,1,1]{2,1,0:T(1,128)} %copy.40), calls=%async_computation.2 | async-start | bytes 65536 | tf_op jit(solution)/shard_map/all_to_all | solution.py:82
  38.2 6.6 %all-to-all-done.2 = s32[64,1,1]{2,1,0:T(1,128)S(1)} async-done(((s32[64,1,1]{2,1,0:T(1,128)}), s32[64,1,1]{2,1,0:T(1,128)S(1)}, u32[]{:S(2)}, u32[]{:S(2)}) %all-to-all-start.2) | async-done | bytes 288 | tf_op jit(solution)/shard_map/all_to_all | solution.py:82
  44.9 6.3 all-to-all-start
  55.3 18.0 %all-to-all-done = bf16[64,16,320]{2,1,0:T(8,128)(2,1)S(1)} async-done(((bf16[64,16,320]{2,1,0:T(8,128)(2,1)}), bf16[64,16,320]{2,1,0:T(8,128)(2,1)S(1)}, u32[]{:S(2)}, u32[]{:S(2)}) %all-to-all-start) | async-done | bytes 655392 | tf_op jit(solution)/shard_map/all_to_all | solution.py:80
  73.9 23.5 %all-reduce.3 = (f32[1024]{0:T(1024)S(1)}, f32[1024]{0:T(1024)S(1)}) all-reduce(f32[1024]{0:T(1024)S(1)} %get-tuple-element.42, f32[1024]{0:T(1024)S(1)} %get-tuple-element.41), channel_id=1, replica_groups=mesh['x'=4,'y'=8,'c'=2,'mp'=8] {'mp'}, use_global_device_ids=true, to_apply=%region_3.5 | all-reduce | flops 2048 | bytes 16384 | tf_op jit(solution)/shard_map/psum | solution.py:99
  99.1 52.7 %all_gather.18 = bf16[1536,192]{1,0:T(8,128)(2,1)} all-gather(bf16[24,192]{1,0:T(8,128)(2,1)S(1)} %copy-done.11), channel_id=1, replica_groups=mesh['x'=4,'y'=8,'c'=2,'mp'=8] {'x','y','c'}, dimensions={0}, use_global_device_ids=true | all-gather | bytes 599040 | tf_op jit(solution)/shard_map/all_gather | solution.py:128
  151.7 3.5 all-to-all-start.3
  157.5 29.9 %all-to-all-done.3 = bf16[8,192,192]{2,1,0:T(8,128)(2,1)S(1)} async-done(((bf16[8,192,192]{2,1,0:T(8,128)(2,1)}), bf16[8,192,192]{2,1,0:T(8,128)(2,1)S(1)}, u32[]{:S(2)}, u32[]{:S(2)}) %all-to-all-start.3) | async-done | bytes 589856 | tf_op jit(solution)/shard_map/all_to_all | solution.py:137
  189.3 4.9 copy.42
  194.2 12.3 %all-gather.5.cloned.1.call-done = bf16[1024,1536]{0,1:T(8,128)(2,1)} async-done(((bf16[1024,192]{0,1:T(8,128)(2,1)}), bf16[1024,1536]{0,1:T(8,128)(2,1)}) %all-gather.5.cloned.1.call-update) | async-done | bytes 3145744 | tf_op jit(solution)/shard_map/all_gather | solution.py:107
  206.5 3.6 fusion.82
  210.7 6.3 fusion.3
  218.6 3.2 all-reduce.9
  221.7 15.9 %all-reduce.5 = (f32[192]{0:T(256)}, f32[]{:T(128)}, f32[192]{0:T(256)}) all-reduce(f32[192]{0:T(256)} %get-tuple-element.57, f32[]{:T(128)} %get-tuple-element.58, f32[192]{0:T(256)} %get-tuple-element.59), channel_id=1, replica_groups=mesh['x'=4,'y'=8,'c'=2,'mp'=8] {'y'}, use_global_device_ids=true, to_apply=%region_6.8 | all-reduce | flops 385 | bytes 3080 | tf_op jit(solution)/shard_map/psum | solution.py:49
  237.7 10.5 %all-reduce.7 = (f32[192]{0:T(256)}, f32[]{:T(128)}, f32[192]{0:T(256)}) all-reduce(f32[192]{0:T(256)} %get-tuple-element.47, f32[]{:T(128)} %get-tuple-element.48, f32[192]{0:T(256)} %get-tuple-element.49), channel_id=1, replica_groups=mesh['x'=4,'y'=8,'c'=2,'mp'=8] {'x'}, use_global_device_ids=true, to_apply=%region_7.9 | all-reduce | flops 385 | bytes 3080 | tf_op jit(solution)/shard_map/psum | solution.py:49
  250.1 4.0 all-gather.11.cloned.1.call-done
  254.1 4.5 fusion.77
  258.7 3.1 all-reduce.8
  261.8 15.5 %all-reduce.4 = (f32[192]{0:T(256)}, f32[192]{0:T(256)}) all-reduce(f32[192]{0:T(256)} %get-tuple-element.55, f32[192]{0:T(256)} %get-tuple-element.56), channel_id=1, replica_groups=mesh['x'=4,'y'=8,'c'=2,'mp'=8] {'y'}, use_global_device_ids=true, to_apply=%region_22.24 | all-reduce | flops 384 | bytes 3072 | tf_op jit(solution)/shard_map/psum | solution.py:49
  277.3 11.1 %all-reduce.6 = (f32[192]{0:T(256)}, f32[192]{0:T(256)}) all-reduce(f32[192]{0:T(256)} %get-tuple-element.45, f32[192]{0:T(256)} %get-tuple-element.46), channel_id=1, replica_groups=mesh['x'=4,'y'=8,'c'=2,'mp'=8] {'x'}, use_global_device_ids=true, to_apply=%region_23.25 | all-reduce | flops 384 | bytes 3072 | tf_op jit(solution)/shard_map/psum | solution.py:49
  289.7 4.1 multiply_reduce_fusion.31
  295.4 4.3 fusion.55
  303.6 3.2 fusion.67
  307.1 31.1 %all-gather.9.cloned.1.call-done = bf16[1024,1536]{0,1:T(8,128)(2,1)} async-done(((bf16[1024,192]{0,1:T(8,128)(2,1)}), bf16[1024,1536]{0,1:T(8,128)(2,1)}) %all-gather.9.cloned.1.call-update) | async-done | bytes 3145744 | tf_op jit(solution)/shard_map/all_gather | solution.py:129
  338.2 4.0 fusion.81
  347.0 3.4 psum.157
  350.5 27.6 %psum.158 = f32[31,192]{1,0:T(8,128)S(1)} all-reduce(f32[31,192]{1,0:T(8,128)S(1)} %psum.157), channel_id=1, replica_groups=mesh['x'=4,'y'=8,'c'=2,'mp'=8] {'y'}, use_global_device_ids=true, to_apply=%region_58.60 | all-reduce | flops 5952 | bytes 47616 | tf_op jit(solution)/shard_map/psum | solution.py:49
  378.0 17.6 %psum.159 = f32[31,192]{1,0:T(8,128)} all-reduce(f32[31,192]{1,0:T(8,128)S(1)} %psum.158), channel_id=1, replica_groups=mesh['x'=4,'y'=8,'c'=2,'mp'=8] {'x'}, use_global_device_ids=true, to_apply=%region_59.61 | all-reduce | flops 5952 | bytes 47616 | tf_op jit(solution)/shard_map/psum | solution.py:49
  395.6 87.4 %reduce-scatter.7.cloned.1.call-done = f32[24,384]{1,0:T(8,128)} async-done(((f32[1536,384]{1,0:T(8,128)}), f32[24,384]{1,0:T(8,128)}) %reduce-scatter.7.cloned.1.call-update) | async-done | bytes 36880
  484.5 3.7 fusion.2
  488.2 147.6 %reduce-scatter.5.cloned.1.call-done = f32[24,192]{1,0:T(8,128)} async-done(((f32[1536,192]{1,0:T(8,128)}), f32[24,192]{1,0:T(8,128)}) %reduce-scatter.5.cloned.1.call-update) | async-done | bytes 18448 | tf_op jit(solution)/shard_map/reduce_scatter | solution.py:133
  (86 shorter events, 39.8 us)
Async XLA Ops:
  7.2 66.3 %copy-start = (bf16[320,192]{0,1:T(8,128)(2,1)S(1)}, bf16[320,192]{0,1:T(8,128)(2,1)}, u32[]{:S(2)}) copy-start(bf16[320,192]{0,1:T(8,128)(2,1)} %param.19) | copy-start | bytes 368644
  10.7 18.1 %all-to-all-start.1 = ((s32[64,1,1]{2,1,0:T(1,128)}), s32[64,1,1]{2,1,0:T(1,128)S(1)}, u32[]{:S(2)}, u32[]{:S(2)}) async-start(s32[64,1,1]{2,1,0:T(1,128)} %copy.39), calls=%async_computation.1 | async-start | bytes 65536 | tf_op jit(solution)/shard_map/all_to_all | solution.py:81
  25.4 29.2 %copy-start.9 = (bf16[128,192]{0,1:T(8,128)(2,1)S(1)}, bf16[128,192]{0,1:T(8,128)(2,1)}, u32[]{:S(2)}) copy-start(bf16[128,192]{0,1:T(8,128)(2,1)} %param.20) | copy-start | bytes 147460
  28.8 16.1 %all-to-all-start.2 = ((s32[64,1,1]{2,1,0:T(1,128)}), s32[64,1,1]{2,1,0:T(1,128)S(1)}, u32[]{:S(2)}, u32[]{:S(2)}) async-start(s32[64,1,1]{2,1,0:T(1,128)} %copy.40), calls=%async_computation.2 | async-start | bytes 65536 | tf_op jit(solution)/shard_map/all_to_all | solution.py:82
  44.9 28.4 %all-to-all-start = ((bf16[64,16,320]{2,1,0:T(8,128)(2,1)}), bf16[64,16,320]{2,1,0:T(8,128)(2,1)S(1)}, u32[]{:S(2)}, u32[]{:S(2)}) async-start(bf16[64,16,320]{2,1,0:T(8,128)(2,1)} %broadcast_select_fusion), calls=%async_computation | async-start | bytes 1572864 | tf_op jit(solution)/shard_map/all_to_all | solution.py:80
  51.2 138.1 %all-gather.7.cloned.1.call-start = ((), (), s32[]{:S(2)}) async-start(), calls=%async_computation.7 | async-start | bytes 1597440 | tf_op jit(solution)/shard_map/all_gather | solution.py:105
  52.0 154.6 %all-gather.5.cloned.1.call-start = ((), (), s32[]{:S(2)}) async-start(), calls=%async_computation.6 | async-start | bytes 3538944 | tf_op jit(solution)/shard_map/all_gather | solution.py:107
  53.3 1.3 copy-start.5
  53.4 1.2 copy-start.6
  54.9 42.5 %copy-start.13 = (f32[192]{0:T(256)S(1)}, f32[192]{0:T(256)}, u32[]{:S(2)}) copy-start(f32[192]{0:T(256)} %param.21) | copy-start | bytes 2308
  55.3 43.8 %copy-start.11 = (bf16[24,192]{1,0:T(8,128)(2,1)S(1)}, bf16[24,192]{1,0:T(8,128)(2,1)}, u32[]{:S(2)}) copy-start(bf16[24,192]{1,0:T(8,128)(2,1)} %param.26) | copy-start | bytes 27652
  73.5 82.0 %copy-start.10 = (f32[31,192]{1,0:T(8,128)S(1)}, f32[31,192]{1,0:T(8,128)}, u32[]{:S(2)}) copy-start(f32[31,192]{1,0:T(8,128)} %param.23) | copy-start | bytes 71428
  73.9 115.4 %copy-start.2 = (f32[1024,192]{0,1:T(8,128)}, f32[1024,192]{0,1:T(8,128)S(1)}, u32[]{:S(2)}) copy-start(f32[1024,192]{0,1:T(8,128)S(1)} %get-tuple-element.103) | copy-start | bytes 2359300
  98.3 155.8 %all-gather.11.cloned.1.call-start = ((), (), s32[]{:S(2)}) async-start(), calls=%async_computation.9 | async-start | bytes 3538944 | tf_op jit(solution)/shard_map/all_gather | solution.py:136
  151.7 35.6 %all-to-all-start.3 = ((bf16[8,192,192]{2,1,0:T(8,128)(2,1)}), bf16[8,192,192]{2,1,0:T(8,128)(2,1)S(1)}, u32[]{:S(2)}, u32[]{:S(2)}) async-start(bf16[8,192,192]{2,1,0:T(8,128)(2,1)} %bitcast.41), calls=%async_computation.3 | async-start | bytes 1572864 | tf_op jit(solution)/shard_map/all_to_all | solution.py:137
  155.3 182.9 %all-gather.9.cloned.1.call-start = ((), (), s32[]{:S(2)}) async-start(), calls=%async_computation.8 | async-start | bytes 3538944 | tf_op jit(solution)/shard_map/all_gather | solution.py:129
  206.5 3.6 copy-start.7
  210.2 83.6 %copy-start.1 = (f32[1024,384]{0,1:T(8,128)}, f32[1024,384]{0,1:T(8,128)S(1)}, u32[]{:S(2)}) copy-start(f32[1024,384]{0,1:T(8,128)S(1)} %fusion.82) | copy-start | bytes 4718596
  293.8 7.2 %copy-start.8 = (f32[1024]{0:T(1024)S(1)}, f32[1024]{0:T(1024)}, u32[]{:S(2)}) copy-start(f32[1024]{0:T(1024)} %copy-done.6) | copy-start | bytes 12292
  293.8 189.2 %reduce-scatter.7.cloned.1.call-start = ((), (), s32[]{:S(2)}) async-start(), calls=%async_computation.11 | async-start | bytes 2396160
  301.0 2.6 copy-start.14
  303.6 34.6 %copy-start.4 = (bf16[1024,192]{0,1:T(8,128)(2,1)S(1)}, bf16[1024,192]{0,1:T(8,128)(2,1)}, u32[]{:S(2)}) copy-start(bf16[1024,192]{0,1:T(8,128)(2,1)} %param.27) | copy-start | bytes 1179652
  306.8 328.9 %reduce-scatter.5.cloned.1.call-start = ((), (), s32[]{:S(2)}) async-start(), calls=%async_computation.10 | async-start | bytes 1597440 | tf_op jit(solution)/shard_map/reduce_scatter | solution.py:133
  342.2 4.7 copy-start.12
  342.2 142.3 %copy-start.3 = (f32[1024,192]{0,1:T(8,128)S(1)}, f32[1024,192]{0,1:T(8,128)}, u32[]{:S(2)}) copy-start(f32[1024,192]{0,1:T(8,128)} %copy-done.2) | copy-start | bytes 2359300
Sparse Core Ops, SparseCore 0:
  55.4 86.5 all-gather.6
  144.6 61.8 all-gather.4
  208.6 45.4 all-gather.10
  294.0 44.1 all-gather.8
  342.8 140.2 reduce-scatter.6
  488.1 147.6 reduce-scatter.4
where the time goes:
time: 644 us; the launch traced here: 643 us
  waiting for transfers between devices  340 us (53%)
  blocking collectives  184 us (29%)
  other arithmetic  32.3 us (5%)
  starting transfers between devices  29.4 us (5%)
  local copies, waits for them, and re-layouts  22.4 us (3%)
  matrix products  19.7 us (3%)
  between operations  14.4 us (2%)
    reduce_scatter x1, waiting for transfers between devices, on_device(): lax.psum_scatter(contract_rows(hidden_full, cotangent), DP_AXES, scatter_...  148 us
    psum x9, blocking collectives, dp_sum(): value = lax.psum(value, name)  108 us
    unnamed x7, waiting for transfers between devices  88.9 us
    all_gather x1, blocking collectives, on_device(): weights_two = lax.all_gather(w_pw2, DP_AXES, axis=0, tiled=True)  52.7 us
    all_gather x1, waiting for transfers between devices, on_device(): hidden_full = lax.all_gather(hidden, 'mp', axis=1, tiled=True)  31.1 us
    all_to_all x1, waiting for transfers between devices, on_device(): lax.all_to_all(weights_two, 'mp', split_axis=0, concat_axis=1, tiled=True)  29.9 us
    psum x1, blocking collectives, on_device(): lax.psum((jnp.sum(inputs, 1), jnp.sum(inputs * inputs, 1)), 'mp')  23.5 us
    all_to_all x1, waiting for transfers between devices, on_device(): lax.all_to_all(blocks, DP_AXES, split_axis=0, concat_axis=0, tiled=True)  18 us
  transfers between devices with their start and end apart: 10, of which 9 were waited for; matrix products, arithmetic and copies ran while one was open for 9% of the time, Pallas kernels for 0%

commit v1 on v0

--- a/solution.py
+++ b/solution.py
@@ -4,6 +4,12 @@
 from jax.sharding import Mesh, PartitionSpec as P
 
 EPS = 1e-05
+
+
+def laid_out(blocks, dim):
+    blocks = jnp.moveaxis(blocks, 0, dim)
+    lengths = blocks.shape
+    return blocks.reshape(*lengths[:dim], lengths[dim] * lengths[dim + 1], *lengths[dim + 2 :])
 
 
 def depth_conv(values, taps, frames):
@@ -126,7 +132,19 @@
     act_sig = jax.nn.sigmoid(act)
     hidden = (valid_col * act * act_sig).astype(jnp.bfloat16)
     weights_two = lax.all_gather(w_pw2, DP_AXES, axis=0, tiled=True)
-    hidden_full = lax.all_gather(hidden, "mp", axis=1, tiled=True)
+    size = lax.axis_size("mp")
+    pairs = [(i, (i + 1) % size) for i in range(size)]
+    back = [(b, a) for a, b in pairs]
+    lower, upper = ([], [])
+    for step_2 in range(size - 1):
+        if step_2 % 2 == 0:
+            lower.append(lax.ppermute(lower[-1] if lower else hidden, "mp", pairs))
+        else:
+            upper.append(lax.ppermute(upper[-1] if upper else hidden, "mp", back))
+    parts = jnp.stack([*lower[::-1], hidden, *upper])
+    shift = lax.axis_index("mp") - len(lower)
+    parts = parts[(jnp.arange(size) - shift) % size]
+    hidden_full = laid_out(parts, 1)
     encoded = (
         inputs + jnp.dot(hidden_full, weights_two, preferred_element_type=jnp.float32)
     ).astype(jnp.bfloat16)

time: 644 us -> 608 us (0.944)
  waiting for transfers between devices: 340 us -> 263 us
  starting transfers between devices: 29.4 us -> 53.2 us
  local copies, waits for them, and re-layouts: 22.4 us -> 40.4 us
    unnamed x7 -> x6, waiting for transfers between devices: 88.9 us -> 19.7 us
    all_gather x1 -> x0, waiting for transfers between devices: 31.1 us -> none  [on_device(): hidden_full = lax.all_gather(hidden, 'mp', axis=1, tiled=True)]
    ppermute x0 -> x7, starting transfers between devices: none -> 24.1 us  [the longest x3 15.7 us: on_device(): upper.append(lax.ppermute(upper[-1] if upper else hidden, 'mp', back))]
    ppermute x0 -> x7, waiting for transfers between devices: none -> 19.9 us  [the longest x4 19.9 us: on_device(): lower.append(lax.ppermute(lower[-1] if lower else hidden, 'mp', pairs))]
    unnamed x31 -> x51, local copies, waits for them, and re-layouts: 2.66 us -> 14.2 us
  transfers between devices with their start and end apart: 10 -> 16, of which waited for: 9 -> 12; matrix products, arithmetic and copies ran while one was open for 9% -> 11% of each run, Pallas kernels for 0% -> 0%
where the time goes in v1:
time: 608 us; the launch traced here: 607 us
  waiting for transfers between devices  263 us (43%)
  blocking collectives  182 us (30%)
  starting transfers between devices  53.2 us (9%)
  local copies, waits for them, and re-layouts  40.4 us (7%)
  other arithmetic  33.7 us (6%)
  matrix products  19.8 us (3%)
  between operations  14.2 us (2%)
    reduce_scatter x1, waiting for transfers between devices, on_device(): lax.psum_scatter(contract_rows(hidden_full, cotangent), DP_AXES, scatter_...  151 us
    psum x9, blocking collectives, dp_sum(): value = lax.psum(value, name)  107 us
    all_gather x1, blocking collectives, on_device(): weights_two = lax.all_gather(w_pw2, DP_AXES, axis=0, tiled=True)  52.4 us
    all_to_all x1, waiting for transfers between devices, on_device(): lax.all_to_all(weights_two, 'mp', split_axis=0, concat_axis=1, tiled=True)  29.8 us
    psum x1, blocking collectives, on_device(): lax.psum((jnp.sum(inputs, 1), jnp.sum(inputs * inputs, 1)), 'mp')  23.5 us
    ppermute x4, waiting for transfers between devices, on_device(): lower.append(lax.ppermute(lower[-1] if lower else hidden, 'mp', pairs))  19.9 us
    unnamed x6, waiting for transfers between devices  19.7 us
    all_to_all x1, waiting for transfers between devices, on_device(): lax.all_to_all(blocks, DP_AXES, split_axis=0, concat_axis=0, tiled=True)  17.4 us
  transfers between devices with their start and end apart: 16, of which 12 were waited for; matrix products, arithmetic and copies ran while one was open for 11% of the time, Pallas kernels for 0%

profile of v1, /device:TPU:16, one launch (start us, length us, event | category | flops | bytes accessed | tf_op | source)
XLA Modules:
  0.0 606.6 jit_solution(6586741862130417409)
XLA Ops:
  10.7 10.5 %all-to-all-start.1 = ((s32[64,1,1]{2,1,0:T(1,128)}), s32[64,1,1]{2,1,0:T(1,128)S(1)}, u32[]{:S(2)}, u32[]{:S(2)}) async-start(s32[64,1,1]{2,1,0:T(1,128)} %copy.41), calls=%async_computation.1 | async-start | bytes 65536 | tf_op jit(solution)/shard_map/all_to_all | solution.py:87
  28.8 8.4 %all-to-all-start.2 = ((s32[64,1,1]{2,1,0:T(1,128)}), s32[64,1,1]{2,1,0:T(1,128)S(1)}, u32[]{:S(2)}, u32[]{:S(2)}) async-start(s32[64,1,1]{2,1,0:T(1,128)} %copy.42), calls=%async_computation.2 | async-start | bytes 65536 | tf_op jit(solution)/shard_map/all_to_all | solution.py:88
  38.2 6.6 %all-to-all-done.2 = s32[64,1,1]{2,1,0:T(1,128)S(1)} async-done(((s32[64,1,1]{2,1,0:T(1,128)}), s32[64,1,1]{2,1,0:T(1,128)S(1)}, u32[]{:S(2)}, u32[]{:S(2)}) %all-to-all-start.2) | async-done | bytes 288 | tf_op jit(solution)/shard_map/all_to_all | solution.py:88
  44.9 6.3 %all-to-all-start = ((bf16[64,16,320]{2,1,0:T(8,128)(2,1)}), bf16[64,16,320]{2,1,0:T(8,128)(2,1)S(1)}, u32[]{:S(2)}, u32[]{:S(2)}) async-start(bf16[64,16,320]{2,1,0:T(8,128)(2,1)} %broadcast_select_fusion), calls=%async_computation | async-start | bytes 1572864 | tf_op jit(solution)/shard_map/all_to_all | solution.py:86
  55.9 17.4 %all-to-all-done = bf16[64,16,320]{2,1,0:T(8,128)(2,1)S(1)} async-done(((bf16[64,16,320]{2,1,0:T(8,128)(2,1)}), bf16[64,16,320]{2,1,0:T(8,128)(2,1)S(1)}, u32[]{:S(2)}, u32[]{:S(2)}) %all-to-all-start) | async-done | bytes 655392 | tf_op jit(solution)/shard_map/all_to_all | solution.py:86
  73.9 23.5 %all-reduce.3 = (f32[1024]{0:T(1024)S(1)}, f32[1024]{0:T(1024)S(1)}) all-reduce(f32[1024]{0:T(1024)S(1)} %get-tuple-element.42, f32[1024]{0:T(1024)S(1)} %get-tuple-element.41), channel_id=1, replica_groups=mesh['x'=4,'y'=8,'c'=2,'mp'=8] {'mp'}, use_global_device_ids=true, to_apply=%region_3.5 | all-reduce | flops 2048 | bytes 16384 | tf_op jit(solution)/shard_map/psum | solution.py:105
  99.1 52.4 %all_gather.14 = bf16[1536,192]{1,0:T(8,128)(2,1)} all-gather(bf16[24,192]{1,0:T(8,128)(2,1)S(1)} %copy-done.14), channel_id=1, replica_groups=mesh['x'=4,'y'=8,'c'=2,'mp'=8] {'x','y','c'}, dimensions={0}, use_global_device_ids=true | all-gather | bytes 599040 | tf_op jit(solution)/shard_map/all_gather | solution.py:134
  157.2 29.8 %all-to-all-done.3 = bf16[8,192,192]{2,1,0:T(8,128)(2,1)S(1)} async-done(((bf16[8,192,192]{2,1,0:T(8,128)(2,1)}), bf16[8,192,192]{2,1,0:T(8,128)(2,1)S(1)}, u32[]{:S(2)}, u32[]{:S(2)}) %all-to-all-start.3) | async-done | bytes 589856 | tf_op jit(solution)/shard_map/all_to_all | solution.py:155
  189.0 4.9 copy.44
  193.8 12.4 %all-gather.4.cloned.1.call-done = bf16[1024,1536]{0,1:T(8,128)(2,1)} async-done(((bf16[1024,192]{0,1:T(8,128)(2,1)}), bf16[1024,1536]{0,1:T(8,128)(2,1)}) %all-gather.4.cloned.1.call-update) | async-done | bytes 3145744 | tf_op jit(solution)/shard_map/all_gather | solution.py:113
  210.4 6.3 %fusion.3 = (f32[192]{0:T(256)}, f32[192]{0:T(256)}, f32[64,16,192]{2,1,0:T(8,128)}) fusion(f32[64,16]{1,0:T(8,128)} %copy-done.8, f32[192]{0:T(256)} %bitcast.180, f32[192]{0:T(256)} %bitcast.182, f32[192]{0:T(256)} %bitcast.186, f32[192]{0:T(256)} %bitcast.188, f32[192]{0:T(256)} %bitcast.190, f32[192]{0:T(256)} %bitcast.192, f32[192]{0:T(256)} %bitcast.194, ...), kind=kLoop, calls=%fused_computation.72 | loop fusion | flops 12779136 | bytes 1602304 | tf_op jit(solution)/shard_map/reduce_sum | solution.py:123
  221.4 15.9 %all-reduce.5 = (f32[192]{0:T(256)}, f32[]{:T(128)}, f32[192]{0:T(256)}) all-reduce(f32[192]{0:T(256)} %get-tuple-element.57, f32[]{:T(128)} %get-tuple-element.58, f32[192]{0:T(256)} %get-tuple-element.59), channel_id=1, replica_groups=mesh['x'=4,'y'=8,'c'=2,'mp'=8] {'y'}, use_global_device_ids=true, to_apply=%region_6.8 | all-reduce | flops 385 | bytes 3080 | tf_op jit(solution)/shard_map/psum | solution.py:55
  237.4 10.4 %all-reduce.7 = (f32[192]{0:T(256)}, f32[]{:T(128)}, f32[192]{0:T(256)}) all-reduce(f32[192]{0:T(256)} %get-tuple-element.47, f32[]{:T(128)} %get-tuple-element.48, f32[192]{0:T(256)} %get-tuple-element.49), channel_id=1, replica_groups=mesh['x'=4,'y'=8,'c'=2,'mp'=8] {'x'}, use_global_device_ids=true, to_apply=%region_7.9 | all-reduce | flops 385 | bytes 3080 | tf_op jit(solution)/shard_map/psum | solution.py:55
  249.6 3.9 all-gather.8.cloned.1.call-done
  253.5 4.5 fusion.80
  261.2 15.5 %all-reduce.4 = (f32[192]{0:T(256)}, f32[192]{0:T(256)}) all-reduce(f32[192]{0:T(256)} %get-tuple-element.55, f32[192]{0:T(256)} %get-tuple-element.56), channel_id=1, replica_groups=mesh['x'=4,'y'=8,'c'=2,'mp'=8] {'y'}, use_global_device_ids=true, to_apply=%region_22.24 | all-reduce | flops 384 | bytes 3072 | tf_op jit(solution)/shard_map/psum | solution.py:55
  276.7 11.1 %all-reduce.6 = (f32[192]{0:T(256)}, f32[192]{0:T(256)}) all-reduce(f32[192]{0:T(256)} %get-tuple-element.45, f32[192]{0:T(256)} %get-tuple-element.46), channel_id=1, replica_groups=mesh['x'=4,'y'=8,'c'=2,'mp'=8] {'x'}, use_global_device_ids=true, to_apply=%region_23.25 | all-reduce | flops 384 | bytes 3072 | tf_op jit(solution)/shard_map/psum | solution.py:55
  289.1 4.1 multiply_reduce_fusion.31
  294.7 4.4 fusion.55
  308.6 5.6 collective-permute-done
  316.1 5.3 collective-permute-start.4
  321.5 5.0 collective-permute-done.1
  329.1 5.1 collective-permute-start.5
  334.3 6.7 %collective-permute-done.2 = bf16[1024,192]{0,1:T(8,128)(2,1)} collective-permute-done((bf16[1024,192]{0,1:T(8,128)(2,1)S(1)}, bf16[1024,192]{0,1:T(8,128)(2,1)}, u32[]{:S(2)}, u32[]{:S(2)}) %collective-permute-start.2) | collective-permute-done | bytes 393248 | tf_op jit(solution)/shard_map/ppermute | solution.py:141
  344.2 5.3 collective-permute-start.6
  364.9 4.4 gather_fusion.1
  369.2 4.0 fusion.84
  381.5 28.9 %psum.158 = f32[31,192]{1,0:T(8,128)S(1)} all-reduce(f32[31,192]{1,0:T(8,128)S(1)} %psum.157), channel_id=1, replica_groups=mesh['x'=4,'y'=8,'c'=2,'mp'=8] {'y'}, use_global_device_ids=true, to_apply=%region_58.60 | all-reduce | flops 5952 | bytes 47616 | tf_op jit(solution)/shard_map/psum | solution.py:55
  410.4 15.0 %psum.159 = f32[31,192]{1,0:T(8,128)} all-reduce(f32[31,192]{1,0:T(8,128)S(1)} %psum.158), channel_id=1, replica_groups=mesh['x'=4,'y'=8,'c'=2,'mp'=8] {'x'}, use_global_device_ids=true, to_apply=%region_59.61 | all-reduce | flops 5952 | bytes 47616 | tf_op jit(solution)/shard_map/psum | solution.py:55
  425.4 3.7 fusion.2
  429.0 18.3 %reduce-scatter.7.cloned.1.call-done = f32[24,384]{1,0:T(8,128)} async-done(((f32[1536,384]{1,0:T(8,128)}), f32[24,384]{1,0:T(8,128)}) %reduce-scatter.7.cloned.1.call-update) | async-done | bytes 36880
  448.9 151.2 %reduce-scatter.5.cloned.1.call-done = f32[24,192]{1,0:T(8,128)} async-done(((f32[1536,192]{1,0:T(8,128)}), f32[24,192]{1,0:T(8,128)}) %reduce-scatter.5.cloned.1.call-update) | async-done | bytes 18448 | tf_op jit(solution)/shard_map/reduce_scatter | solution.py:151
  (123 shorter events, 85.7 us)
Async XLA Ops:
  7.2 66.3 %copy-start = (bf16[320,192]{0,1:T(8,128)(2,1)S(1)}, bf16[320,192]{0,1:T(8,128)(2,1)}, u32[]{:S(2)}) copy-start(bf16[320,192]{0,1:T(8,128)(2,1)} %param.19) | copy-start | bytes 368644
  10.7 18.1 %all-to-all-start.1 = ((s32[64,1,1]{2,1,0:T(1,128)}), s32[64,1,1]{2,1,0:T(1,128)S(1)}, u32[]{:S(2)}, u32[]{:S(2)}) async-start(s32[64,1,1]{2,1,0:T(1,128)} %copy.41), calls=%async_computation.1 | async-start | bytes 65536 | tf_op jit(solution)/shard_map/all_to_all | solution.py:87
  25.4 29.8 %copy-start.12 = (bf16[128,192]{0,1:T(8,128)(2,1)S(1)}, bf16[128,192]{0,1:T(8,128)(2,1)}, u32[]{:S(2)}) copy-start(bf16[128,192]{0,1:T(8,128)(2,1)} %param.20) | copy-start | bytes 147460
  28.8 16.1 %all-to-all-start.2 = ((s32[64,1,1]{2,1,0:T(1,128)}), s32[64,1,1]{2,1,0:T(1,128)S(1)}, u32[]{:S(2)}, u32[]{:S(2)}) async-start(s32[64,1,1]{2,1,0:T(1,128)} %copy.42), calls=%async_computation.2 | async-start | bytes 65536 | tf_op jit(solution)/shard_map/all_to_all | solution.py:88
  44.9 28.4 %all-to-all-start = ((bf16[64,16,320]{2,1,0:T(8,128)(2,1)}), bf16[64,16,320]{2,1,0:T(8,128)(2,1)S(1)}, u32[]{:S(2)}, u32[]{:S(2)}) async-start(bf16[64,16,320]{2,1,0:T(8,128)(2,1)} %broadcast_select_fusion), calls=%async_computation | async-start | bytes 1572864 | tf_op jit(solution)/shard_map/all_to_all | solution.py:86
  51.2 137.8 %all-gather.6.cloned.1.call-start = ((), (), s32[]{:S(2)}) async-start(), calls=%async_computation.7 | async-start | bytes 1597440 | tf_op jit(solution)/shard_map/all_gather | solution.py:111
  52.0 154.2 %all-gather.4.cloned.1.call-start = ((), (), s32[]{:S(2)}) async-start(), calls=%async_computation.6 | async-start | bytes 3538944 | tf_op jit(solution)/shard_map/all_gather | solution.py:113
  55.5 41.9 %copy-start.20 = (f32[192]{0:T(256)S(1)}, f32[192]{0:T(256)}, u32[]{:S(2)}) copy-start(f32[192]{0:T(256)} %param.21) | copy-start | bytes 2308
  55.8 43.2 %copy-start.14 = (bf16[24,192]{1,0:T(8,128)(2,1)S(1)}, bf16[24,192]{1,0:T(8,128)(2,1)}, u32[]{:S(2)}) copy-start(bf16[24,192]{1,0:T(8,128)(2,1)} %param.26) | copy-start | bytes 27652
  73.5 81.7 %copy-start.13 = (f32[31,192]{1,0:T(8,128)S(1)}, f32[31,192]{1,0:T(8,128)}, u32[]{:S(2)}) copy-start(f32[31,192]{1,0:T(8,128)} %param.23) | copy-start | bytes 71428
  73.9 115.0 %copy-start.4 = (f32[1024,192]{0,1:T(8,128)}, f32[1024,192]{0,1:T(8,128)S(1)}, u32[]{:S(2)}) copy-start(f32[1024,192]{0,1:T(8,128)S(1)} %get-tuple-element.103) | copy-start | bytes 2359300
  98.3 155.2 %all-gather.8.cloned.1.call-start = ((), (), s32[]{:S(2)}) async-start(), calls=%async_computation.8 | async-start | bytes 3538944 | tf_op jit(solution)/shard_map/all_gather | solution.py:154
  151.4 35.6 %all-to-all-start.3 = ((bf16[8,192,192]{2,1,0:T(8,128)(2,1)}), bf16[8,192,192]{2,1,0:T(8,128)(2,1)S(1)}, u32[]{:S(2)}, u32[]{:S(2)}) async-start(bf16[8,192,192]{2,1,0:T(8,128)(2,1)} %bitcast.52), calls=%async_computation.3 | async-start | bytes 1572864 | tf_op jit(solution)/shard_map/all_to_all | solution.py:155
  155.0 292.4 %reduce-scatter.7.cloned.1.call-start = ((), (), s32[]{:S(2)}) async-start(), calls=%async_computation.10 | async-start | bytes 2396160
  209.9 83.4 %copy-start.1 = (f32[1024,384]{0,1:T(8,128)}, f32[1024,384]{0,1:T(8,128)S(1)}, u32[]{:S(2)}) copy-start(f32[1024,384]{0,1:T(8,128)S(1)} %fusion.85) | copy-start | bytes 4718596
  293.3 7.1 %copy-start.11 = (f32[1024]{0:T(1024)S(1)}, f32[1024]{0:T(1024)}, u32[]{:S(2)}) copy-start(f32[1024]{0:T(1024)} %copy-done.9) | copy-start | bytes 12292
  300.4 4.8 copy-start.21
  302.5 11.7 %collective-permute-start = (bf16[1024,192]{0,1:T(8,128)(2,1)}, bf16[1024,192]{0,1:T(8,128)(2,1)}, u32[]{:S(2)}, u32[]{:S(2)}) collective-permute-start(bf16[1024,192]{0,1:T(8,128)(2,1)} %get-tuple-element.69), channel_id=1, source_target_pairs={{0,1},{1,2},{2,3},{3,4},{4,5},{5,6},{6,7},{7,0},{8,9},{9,10},{10,1... | collective-permute-start | bytes 1179656 | tf_op jit(solution)/shard_map/ppermute | solution.py:141
  305.2 37.7 %copy-start.2 = (f32[64,16,192]{2,1,0:T(8,128)S(1)}, f32[64,16,192]{2,1,0:T(8,128)}, u32[]{:S(2)}) copy-start(f32[64,16,192]{2,1,0:T(8,128)} %get-tuple-element.64) | copy-start | bytes 2359300
  308.5 50.7 %copy-start.15 = (f32[192]{0:T(256)S(1)}, f32[192]{0:T(256)}, u32[]{:S(2)}) copy-start(f32[192]{0:T(256)} %get-tuple-element.62) | copy-start | bytes 2308
  308.5 50.7 %copy-start.16 = (f32[192]{0:T(256)S(1)}, f32[192]{0:T(256)}, u32[]{:S(2)}) copy-start(f32[192]{0:T(256)} %get-tuple-element.63) | copy-start | bytes 2308
  308.5 50.7 %copy-start.17 = (f32[192]{0:T(256)S(1)}, f32[192]{0:T(256)}, u32[]{:S(2)}) copy-start(f32[192]{0:T(256)} %param.25) | copy-start | bytes 2308
  308.5 50.7 %copy-start.18 = (f32[192]{0:T(256)S(1)}, f32[192]{0:T(256)}, u32[]{:S(2)}) copy-start(f32[192]{0:T(256)} %param.24) | copy-start | bytes 2308
  308.5 291.5 %reduce-scatter.5.cloned.1.call-start = ((), (), s32[]{:S(2)}) async-start(), calls=%async_computation.9 | async-start | bytes 1597440 | tf_op jit(solution)/shard_map/reduce_scatter | solution.py:151
  314.2 12.3 %collective-permute-start.1 = (bf16[1024,192]{0,1:T(8,128)(2,1)}, bf16[1024,192]{0,1:T(8,128)(2,1)S(1)}, u32[]{:S(2)}, u32[]{:S(2)}) collective-permute-start(bf16[1024,192]{0,1:T(8,128)(2,1)} %collective-permute-done), channel_id=1, source_target_pairs={{0,1},{1,2},{2,3},{3,4},{4,5},{5,6},{6,7},{7,0},{8,9},{9,10},{10,1... | collective-permute-start | bytes 1179656 | tf_op jit(solution)/shard_map/ppermute | solution.py:141
  316.1 13.0 %collective-permute-start.4 = (bf16[1024,192]{0,1:T(8,128)(2,1)}, bf16[1024,192]{0,1:T(8,128)(2,1)}, u32[]{:S(2)}, u32[]{:S(2)}) collective-permute-start(bf16[1024,192]{0,1:T(8,128)(2,1)} %get-tuple-element.69), channel_id=1, source_target_pairs={{1,0},{2,1},{3,2},{4,3},{5,4},{6,5},{7,6},{0,7},{9,8},{10,9},{11,1... | collective-permute-start | bytes 1179656 | tf_op jit(solution)/shard_map/ppermute | solution.py:143
  327.2 13.7 %collective-permute-start.2 = (bf16[1024,192]{0,1:T(8,128)(2,1)S(1)}, bf16[1024,192]{0,1:T(8,128)(2,1)}, u32[]{:S(2)}, u32[]{:S(2)}) collective-permute-start(bf16[1024,192]{0,1:T(8,128)(2,1)S(1)} %collective-permute-done.1), channel_id=1, source_target_pairs={{0,1},{1,2},{2,3},{3,4},{4,5},{5,6},{6,7},{7,0},{8,9},{9,10},{10,1... | collective-permute-start | bytes 1179656 | tf_op jit(solution)/shard_map/ppermute | solution.py:141
  329.1 15.1 %collective-permute-start.5 = (bf16[1024,192]{0,1:T(8,128)(2,1)}, bf16[1024,192]{0,1:T(8,128)(2,1)}, u32[]{:S(2)}, u32[]{:S(2)}) collective-permute-start(bf16[1024,192]{0,1:T(8,128)(2,1)} %collective-permute-done.4), channel_id=1, source_target_pairs={{1,0},{2,1},{3,2},{4,3},{5,4},{6,5},{7,6},{0,7},{9,8},{10,9},{11,1... | collective-permute-start | bytes 1179656 | tf_op jit(solution)/shard_map/ppermute | solution.py:143
  340.9 11.2 %collective-permute-start.3 = (bf16[1024,192]{0,1:T(8,128)(2,1)}, bf16[1024,192]{0,1:T(8,128)(2,1)}, u32[]{:S(2)}, u32[]{:S(2)}) collective-permute-start(bf16[1024,192]{0,1:T(8,128)(2,1)} %collective-permute-done.2), channel_id=1, source_target_pairs={{0,1},{1,2},{2,3},{3,4},{4,5},{5,6},{6,7},{7,0},{8,9},{9,10},{10,1... | collective-permute-start | bytes 1179656 | tf_op jit(solution)/shard_map/ppermute | solution.py:141
  344.2 15.0 %copy-start.3 = (f32[1,1024,192]{1,2,0:T(8,128)S(1)}, f32[1,1024,192]{1,2,0:T(8,128)}, u32[]{:S(2)}) copy-start(f32[1,1024,192]{1,2,0:T(8,128)} %copy.47) | copy-start | bytes 2359300
  344.2 19.9 %collective-permute-start.6 = (bf16[1024,192]{0,1:T(8,128)(2,1)}, bf16[1024,192]{0,1:T(8,128)(2,1)S(1)}, u32[]{:S(2)}, u32[]{:S(2)}) collective-permute-start(bf16[1024,192]{0,1:T(8,128)(2,1)} %collective-permute-done.5), channel_id=1, source_target_pairs={{1,0},{2,1},{3,2},{4,3},{5,4},{6,5},{7,6},{0,7},{9,8},{10,9},{11,1... | collective-permute-start | bytes 1179656 | tf_op jit(solution)/shard_map/ppermute | solution.py:143
  373.2 52.1 %copy-start.5 = (f32[1024,192]{0,1:T(8,128)S(1)}, f32[1024,192]{0,1:T(8,128)}, u32[]{:S(2)}) copy-start(f32[1024,192]{0,1:T(8,128)} %copy-done.4) | copy-start | bytes 2359300
  (6 other events, 16.3 us)
Sparse Core Ops, SparseCore 0:
  55.4 86.6 all-gather.5
  144.7 61.4 all-gather.3
  208.3 45.2 all-gather.7
  308.6 138.6 reduce-scatter.6
  452.4 147.5 reduce-scatter.4
